TPU v7x, 256 devices: a whole 4x4x8 slice. The times are simulated.
256 devices in a mesh: dp: 16 (over x, y_hi, core), mp: 16 (over y_lo, z).
Axes of the slice: x: 4, y: 4 (y_hi: 2, y_lo: 2; y = y_hi * 2 + y_lo), z: 8, core: 2. Of those that a mesh axis runs over, the one named last changes fastest.
Arguments:
- tokens: bfloat16 [4096, 4096], P('dp'), may hold values from -32 to 32
- weights: bfloat16 [4096, 2, 3, 4096], P('dp', None, None, 'mp'), may hold values from -1 to 1
- block_modality: int32 [32], replicated, may hold values from 0 to 1
- doc_ids: int32 [4096], replicated, may hold values from 0 to 31, never falling along the last dimension, each value on 1 to 1024 neighbouring positions
- grad_out: bfloat16 [4096, 4096], P('dp', 'mp'), may hold values from -6 to 6
Outputs:
- attended: bfloat16 [4096, 4096], P('dp', 'mp')
- grad_tokens: bfloat16 [4096, 4096], P('dp', 'mp')
- grad_weights: bfloat16 [4096, 2, 3, 4096], P('dp', None, None, 'mp')
Inputs may be any that keep to these rules, and one draw needn't show every extreme that they name: doc_ids never falls along the sequence; a document is a run of equal ids of at most 1024 tokens, and one document has exactly 1024.
All inputs are finite; a program needn't handle non-finite values.
Results may differ from a plain program's by a relative error of at most 0.025.
Values may be sent and summed in bfloat16 or wider, within the bound.
No kernel may reach another device: no remote copies, remote signals or barrier semaphores. Data moves between devices by JAX's collectives and lax.ppermute only.
A program may use at most 128 MiB of HBM per device.

v0:
```python
import jax
import jax.numpy as jnp
from jax import lax
from jax.sharding import PartitionSpec as P

HD = 128
BLOCK = 128
SPAN = 4


def shifted(block, axis, distance):
    devices = range(lax.axis_size(axis))
    route = [(i - distance, i) for i in devices if i - distance in devices]
    return lax.ppermute(block, axis, route)


def select_product(block_rows, modality, text_mat, image_mat, contract):
    contraction = (((1,), (contract,)), ((), ()))
    return lax.cond(
        modality == 0,
        lambda: lax.dot_general(
            block_rows, text_mat, contraction, preferred_element_type=jnp.float32
        ),
        lambda: lax.dot_general(
            block_rows, image_mat, contraction, preferred_element_type=jnp.float32
        ),
    )


def blockwise(row_data, modalities, text_mat, image_mat, contract):
    blocks = row_data.reshape(modalities.shape[0], BLOCK, row_data.shape[1])

    def one_block(block_pair):
        return select_product(block_pair[0], block_pair[1], text_mat, image_mat, contract)

    result = lax.map(one_block, (blocks, modalities))
    return result.reshape(row_data.shape[0], result.shape[2])


def on_device(tokens, weights, block_modality, doc_ids, grad_out):
    local_rows = tokens.shape[0]
    width_rows = weights.shape[0]
    head_width = weights.shape[3]
    head_count = head_width // HD
    dp_devices = lax.axis_size("dp")
    local_blocks = local_rows // BLOCK
    front_pad = SPAN * local_rows
    window_len = front_pad + local_rows
    my_index = lax.axis_index("dp")
    scale_factor = HD ** (-0.5)
    my_mods = lax.dynamic_slice_in_dim(block_modality, my_index * local_blocks, local_blocks, 0)
    flat_weights = weights.reshape(width_rows, 2, 3 * head_width)
    text_local = flat_weights[:, 0]
    image_local = flat_weights[:, 1]
    columns = lax.all_to_all(tokens, "dp", split_axis=1, concat_axis=0, tiled=True)
    text_whole, image_whole = (
        lax.all_gather(text_local, "dp", axis=0, tiled=True),
        lax.all_gather(image_local, "dp", axis=0, tiled=True),
    )
    summed = blockwise(tokens, my_mods, text_whole, image_whole, 0)
    qkv = summed.astype(jnp.bfloat16).reshape(local_rows, 3, head_count, HD)
    queries = qkv[:, 0]
    key_values = qkv[:, 1:]
    received = []
    for distance in range(SPAN, 0, -1):
        received.append(shifted(key_values, "dp", distance))
    window = jnp.concatenate(received + [key_values], 0)
    key_rows = window[:, 0]
    value_rows = window[:, 1]
    docs_pad = jnp.concatenate([jnp.full((front_pad,), -1, jnp.int32), doc_ids], 0)
    key_docs = lax.dynamic_slice_in_dim(docs_pad, my_index * local_rows, window_len, 0)
    query_docs = lax.dynamic_slice_in_dim(doc_ids, my_index * local_rows, local_rows, 0)
    offsets = jnp.arange(window_len, dtype=jnp.int32) - front_pad
    allowed = (key_docs[None, :] == query_docs[:, None]) & (
        offsets[None, :] <= jnp.arange(local_rows, dtype=jnp.int32)[:, None]
    )
    scores = (
        jnp.einsum("qhd,khd->hqk", queries, key_rows, preferred_element_type=jnp.float32)
        * scale_factor
    )
    scores = jnp.where(allowed[None], scores, -1e30)
    top_score = jnp.max(scores, axis=-1, keepdims=True)
    expos = jnp.where(allowed[None], jnp.exp(scores - top_score), 0.0)
    probs_f = expos / jnp.sum(expos, axis=-1, keepdims=True)
    probs = probs_f.astype(jnp.bfloat16)
    attended = jnp.einsum("hqk,khd->qhd", probs, value_rows, preferred_element_type=jnp.float32)
    attended = attended.astype(jnp.bfloat16).reshape(local_rows, head_width)
    upstream = grad_out.reshape(local_rows, head_count, HD)
    dprob = jnp.einsum("qhd,khd->hqk", upstream, value_rows, preferred_element_type=jnp.float32)
    row_delta = jnp.sum(probs_f * dprob, axis=-1, keepdims=True)
    dscore = (probs_f * (dprob - row_delta)).astype(jnp.bfloat16)
    grad_q = (
        jnp.einsum("hqk,khd->qhd", dscore, key_rows, preferred_element_type=jnp.float32)
        * scale_factor
    )
    grad_k = (
        jnp.einsum("hqk,qhd->khd", dscore, queries, preferred_element_type=jnp.float32)
        * scale_factor
    )
    grad_v = jnp.einsum("hqk,qhd->khd", probs, upstream, preferred_element_type=jnp.float32)
    window_grads = jnp.stack([grad_k, grad_v], 1)
    own_grads = window_grads[front_pad:]
    for distance in range(1, SPAN + 1):
        lower_edge = front_pad - distance * local_rows
        sent_block = window_grads[lower_edge : lower_edge + local_rows]
        own_grads = own_grads + shifted(sent_block.astype(jnp.bfloat16), "dp", -distance).astype(
            sent_block.dtype
        )
    dqkv = (
        jnp.concatenate([grad_q[:, None], own_grads], 1)
        .astype(jnp.bfloat16)
        .reshape(local_rows, 3 * head_width)
    )
    gathered = lax.all_gather(dqkv, "dp", axis=0, tiled=True)
    column_groups = columns.reshape(dp_devices, local_blocks, BLOCK, width_rows)
    grad_groups = gathered.reshape(dp_devices, local_blocks, BLOCK, 3 * head_width)
    modality_groups = block_modality.reshape(dp_devices, local_blocks)
    modality_range = jnp.arange(2, dtype=jnp.int32)

    def accumulate(running, triple):
        column_group, grad_group, group_mods = triple
        per_block = jnp.einsum(
            "bnf,bnc->bfc", column_group, grad_group, preferred_element_type=jnp.float32
        )
        selector = (group_mods[:, None] == modality_range[None, :]).astype(jnp.float32)
        return (running + jnp.sum(selector[:, :, None, None] * per_block[:, None], axis=0), None)

    weight_sum, unused = lax.scan(
        accumulate,
        jnp.zeros((2, width_rows, 3 * head_width), jnp.float32),
        (column_groups, grad_groups, modality_groups),
    )
    grad_weights = (
        jnp.transpose(weight_sum, (1, 0, 2))
        .astype(jnp.bfloat16)
        .reshape(width_rows, 2, 3, head_width)
    )
    input_terms = blockwise(dqkv, my_mods, text_whole, image_whole, 1)
    grad_tokens = lax.psum_scatter(
        input_terms.astype(jnp.bfloat16), "mp", scatter_dimension=1, tiled=True
    )
    return (attended, grad_tokens, grad_weights)


def solution(mesh):
    return jax.shard_map(
        on_device,
        mesh=mesh,
        in_specs=(P("dp", None), P("dp", None, None, "mp"), P(), P(), P("dp", "mp")),
        out_specs=(P("dp", "mp"), P("dp", "mp"), P("dp", None, None, "mp")),
        check_vma=False,
    )
```

profile of v0, /device:TPU:4, one launch (start us, length us, event | category | flops | bytes accessed | tf_op | source)
XLA Modules:
  0.0 415.7 jit_solution(13535835044259661621)
XLA Ops:
  11.5 74.8 %all-gather.8.cloned.1.call-done = bf16[4096,1,768]{0,2,1:T(8,128)(2,1)} async-done(((bf16[256,1,768]{0,2,1:T(8,128)(2,1)}), bf16[4096,1,768]{0,2,1:T(8,128)(2,1)}) %all-gather.8.cloned.1.call-update) | async-done | bytes 6291472 | tf_op jit(solution)/shard_map/all_gather | solution.py:58
  86.4 8.6 %copy.59 = bf16[4096,768]{1,0:T(8,128)(2,1)} copy(bf16[4096,768]{0,1:T(8,128)(2,1)} %bitcast.114) | data formatting | bytes 12582912 | tf_op jit(solution)/shard_map/while | solution.py:36
  95.0 67.1 %all-gather.10.cloned.1.call-done = bf16[4096,1,768]{0,2,1:T(8,128)(2,1)} async-done(((bf16[256,1,768]{0,2,1:T(8,128)(2,1)}), bf16[4096,1,768]{0,2,1:T(8,128)(2,1)}) %all-gather.10.cloned.1.call-update) | async-done | bytes 6291472 | tf_op jit(solution)/shard_map/all_gather | solution.py:57
  162.1 8.8 %copy.60 = bf16[4096,768]{1,0:T(8,128)(2,1)} copy(bf16[4096,768]{0,1:T(8,128)(2,1)} %bitcast.115) | data formatting | bytes 12582912 | tf_op jit(solution)/shard_map/while | solution.py:36
  170.9 11.7 %while.31 = (s32[]{:T(128)}, bf16[2,128,768]{2,1,0:T(8,128)(2,1)}, s32[2]{0:T(128)S(1)}, bf16[2,128,4096]{2,1,0:T(8,128)(2,1)S(1)}, bf16[4096,768]{1,0:T(8,128)(...) while((s32[]{:T(128)}, bf16[2,128,768]{2,1,0:T(8,128)(2,1)}, s32[2]{0:T(128)S(1)}, ...), condition=%wide.region_3.4_spmd, body=%wide.region_0.3_spmd.sunk | while | flops 805306368 | bytes 10027175 | solution.py:36
  172.2 3.8 conditional.4
  178.1 3.8 conditional.4
  183.9 4.3 %collective-permute-start = (bf16[256,2,2,128]{3,0,2,1:T(8,128)(2,1)S(1)}, bf16[256,2,2,128]{3,0,2,1:T(8,128)(2,1)}, u32[]{:S(2)}, u32[]{:S(2)}) collective-permute-start(bf16[256,2,2,128]{3,0,2,1:T(8,128)(2,1)S(1)} %copy.84), channel_id=1, source_target_pairs={{0,64},{16,80},{32,96},{48,112},{64,128},{80,144},{96,160},{112,17... | collective-permute-start | bytes 786440 | tf_op jit(solution)/shard_map/ppermute | solution.py:14
  190.3 4.0 collective-permute-start.2
  200.8 6.3 %collective-permute-done.2 = bf16[256,2,2,128]{3,0,2,1:T(8,128)(2,1)} collective-permute-done((bf16[256,2,2,128]{3,0,2,1:T(8,128)(2,1)S(1)}, bf16[256,2,2,128]{3,0,2,1:T(8,128)(2,1)}, u32[]{:S(2)}, u32[]{:S(2)}) %collective-permute-start.2) | collective-permute-done | bytes 262176 | tf_op jit(solution)/shard_map/ppermute | solution.py:14
  210.3 4.0 fusion.30
  225.9 4.6 %collective-permute-start.4 = (bf16[256,2,2,128]{0,3,2,1:T(8,128)(2,1)S(1)}, bf16[256,2,2,128]{0,3,2,1:T(8,128)(2,1)S(1)}, u32[]{:S(2)}, u32[]{:S(2)}) collective-permute-start(bf16[256,2,2,128]{0,3,2,1:T(8,128)(2,1)S(1)} %get-tuple-element.257), channel_id=1, source_target_pairs={{16,0},{32,16},{48,32},{64,48},{80,64},{96,80},{112,96},{128,112},... | collective-permute-start | bytes 786440 | tf_op jit(solution)/shard_map/ppermute | solution.py:14
  243.7 7.3 %all-to-all-start = ((bf16[256,16,256]{0,2,1:T(8,128)(2,1)}), bf16[256,16,256]{0,2,1:T(8,128)(2,1)}, u32[]{:S(2)}, u32[]{:S(2)}) async-start(bf16[256,16,256]{0,2,1:T(8,128)(2,1)} %bitcast.113), calls=%async_computation.1 | async-start | bytes 4194304 | tf_op jit(solution)/shard_map/all_to_all | solution.py:55
  251.4 30.8 %all-to-all-done = bf16[256,16,256]{0,2,1:T(8,128)(2,1)} async-done(((bf16[256,16,256]{0,2,1:T(8,128)(2,1)}), bf16[256,16,256]{0,2,1:T(8,128)(2,1)}, u32[]{:S(2)}, u32[]{:S(2)}) %all-to-all-start) | async-done | bytes 2097184 | tf_op jit(solution)/shard_map/all_to_all | solution.py:55
  282.2 3.9 copy.73
  290.1 14.7 %while.32 = (s32[]{:T(128)}, bf16[2,128,4096]{2,1,0:T(8,128)(2,1)}, s32[2]{0:T(128)S(1)}, bf16[2,128,768]{2,1,0:T(8,128)(2,1)S(1)}, bf16[4096,768]{1,0:T(8,128)(...) while((s32[]{:T(128)}, bf16[2,128,4096]{2,1,0:T(8,128)(2,1)}, s32[2]{0:T(128)S(1)}, ...), condition=%wide.region_10.11_spmd, body=%wide.region_7.10_spmd.sunk | while | flops 805306368 | bytes 10027175 | solution.py:36
  291.3 4.9 %conditional.5 = (bf16[1,128,4096]{2,1,0:T(8,128)(2,1)S(1)}) conditional(s32[]{:T(128)} %bitcast.106, (bf16[128,768]{1,0:T(8,128)(2,1)S(1)}, bf16[4096,768]{1,0:T(8,128)(2,1)}) %tuple.94, (bf16[128,768]{1,0:T(8,128)(2,1)S(1)}, bf16[4096,768]{1,0:T(8,128)(2,1)}) %tuple.95), branch_computations={%region_8.8_spmd, %region_9.9_spmd} | conditional | flops 805306368 | bytes 7536648 | solution.py:19
  291.3 4.9 %convolution_bitcast_fusion.3 = bf16[1,128,4096]{2,1,0:T(8,128)(2,1)S(1)} fusion(bf16[128,768]{1,0:T(8,128)(2,1)S(1)} %get-tuple-element.109, bf16[4096,768]{1,0:T(8,128)(2,1)} %get-tuple-element.110), kind=kOutput, calls=%fused_computation.6 | convolution fusion | flops 805306368 | bytes 7536640 | tf_op jit(solution)/shard_map/while/body/eval_jaxpr/cond/branch_1_fun/dot_general | solution.py:21
  298.6 5.1 %conditional.5 = (bf16[1,128,4096]{2,1,0:T(8,128)(2,1)S(1)}) conditional(s32[]{:T(128)} %bitcast.106, (bf16[128,768]{1,0:T(8,128)(2,1)S(1)}, bf16[4096,768]{1,0:T(8,128)(2,1)}) %tuple.94, (bf16[128,768]{1,0:T(8,128)(2,1)S(1)}, bf16[4096,768]{1,0:T(8,128)(2,1)}) %tuple.95), branch_computations={%region_8.8_spmd, %region_9.9_spmd} | conditional | flops 805306368 | bytes 7536648 | solution.py:19
  298.6 5.1 %convolution_bitcast_fusion.3 = bf16[1,128,4096]{2,1,0:T(8,128)(2,1)S(1)} fusion(bf16[128,768]{1,0:T(8,128)(2,1)S(1)} %get-tuple-element.109, bf16[4096,768]{1,0:T(8,128)(2,1)} %get-tuple-element.110), kind=kOutput, calls=%fused_computation.6 | convolution fusion | flops 805306368 | bytes 7536640 | tf_op jit(solution)/shard_map/while/body/eval_jaxpr/cond/branch_1_fun/dot_general | solution.py:21
  304.8 26.7 %all-gather.6.cloned.1.call-done = bf16[4096,768]{0,1:T(8,128)(2,1)} async-done(((bf16[256,768]{0,1:T(8,128)(2,1)}), bf16[4096,768]{0,1:T(8,128)(2,1)}) %all-gather.6.cloned.1.call-update) | async-done | bytes 6291472 | tf_op jit(solution)/shard_map/all_gather | solution.py:114
  331.5 8.6 %copy.74 = bf16[4096,768]{1,0:T(8,128)(2,1)} copy(bf16[4096,768]{0,1:T(8,128)(2,1)} %all-gather.6.cloned.1.call-done) | data formatting | bytes 12582912 | tf_op jit(solution)/shard_map/all_gather | solution.py:114
  340.1 39.0 %while.33 = (s32[]{:T(128)}, f32[2,256,768]{2,1,0:T(8,128)S(1)}, s32[16,2]{1,0:T(8,128)S(1)}, bf16[16,2,128,256]{3,2,1,0:T(8,128)(2,1)}, bf16[16,2,128,768]{3,2,1,0:T(8,128)(2,1)}, /*index=5*/s32[]{:T(128)}, s32[]{:T(128)}) while((s32[]{:T(128)}, f32[2,256,768]{2,1,0:T(8,128)S(1)}, s32[16,2]{1,0:T(8,128)S(1)}, ...), condition=%wide.region_14.15_spmd.clone, body=%wide.region_12.14_spmd.clone.sunk | while | flops 102629384 | bytes 9962651 | solution.py:128
  381.3 27.9 %reduce-scatter.2.cloned.1.call-done = bf16[256,256]{1,0:T(8,128)(2,1)} async-done(((bf16[256,4096]{1,0:T(8,128)(2,1)}), bf16[256,256]{1,0:T(8,128)(2,1)}) %reduce-scatter.2.cloned.1.call-update) | async-done | bytes 131088 | tf_op jit(solution)/shard_map/reduce_scatter | solution.py:139
  (164 shorter events, 100.4 us)
Async XLA Ops:
  7.2 4.1 copy-start.6
  7.2 4.2 %copy-start.5 = (s32[4096]{0:T(1024)S(1)}, s32[4096]{0:T(1024)}, u32[]{:S(2)}) copy-start(s32[4096]{0:T(1024)} %param.18) | copy-start | bytes 49156
  7.2 79.2 %all-gather.8.cloned.1.call-start = ((), (), s32[]{:S(2)}) async-start(), calls=%async_computation.4 | async-start | bytes 6684672 | tf_op jit(solution)/shard_map/all_gather | solution.py:58
  10.5 151.6 %all-gather.10.cloned.1.call-start = ((), (), s32[]{:S(2)}) async-start(), calls=%async_computation.5 | async-start | bytes 6684672 | tf_op jit(solution)/shard_map/all_gather | solution.py:57
  11.2 320.3 %all-gather.6.cloned.1.call-start = ((), (), s32[]{:S(2)}) async-start(), calls=%async_computation.3 | async-start | bytes 6684672 | tf_op jit(solution)/shard_map/all_gather | solution.py:114
  162.1 8.8 %copy-start = (bf16[256,4096]{1,0:T(8,128)(2,1)S(1)}, bf16[256,4096]{1,0:T(8,128)(2,1)}, u32[]{:S(2)}) copy-start(bf16[256,4096]{1,0:T(8,128)(2,1)} %param.15) | copy-start | bytes 6291460
  182.6 12.0 %copy-start.3 = (bf16[256,256]{1,0:T(8,128)(2,1)S(1)}, bf16[256,256]{1,0:T(8,128)(2,1)}, u32[]{:S(2)}) copy-start(bf16[256,256]{1,0:T(8,128)(2,1)} %param.19) | copy-start | bytes 393220
  183.9 13.4 %collective-permute-start = (bf16[256,2,2,128]{3,0,2,1:T(8,128)(2,1)S(1)}, bf16[256,2,2,128]{3,0,2,1:T(8,128)(2,1)}, u32[]{:S(2)}, u32[]{:S(2)}) collective-permute-start(bf16[256,2,2,128]{3,0,2,1:T(8,128)(2,1)S(1)} %copy.84), channel_id=1, source_target_pairs={{0,64},{16,80},{32,96},{48,112},{64,128},{80,144},{96,160},{112,17... | collective-permute-start | bytes 786440 | tf_op jit(solution)/shard_map/ppermute | solution.py:14
  188.2 10.9 %collective-permute-start.1 = (bf16[256,2,2,128]{3,0,2,1:T(8,128)(2,1)S(1)}, bf16[256,2,2,128]{3,0,2,1:T(8,128)(2,1)}, u32[]{:S(2)}, u32[]{:S(2)}) collective-permute-start(bf16[256,2,2,128]{3,0,2,1:T(8,128)(2,1)S(1)} %copy.84), channel_id=1, source_target_pairs={{0,48},{16,64},{32,80},{48,96},{64,112},{80,128},{96,144},{112,160... | collective-permute-start | bytes 786440 | tf_op jit(solution)/shard_map/ppermute | solution.py:14
  190.3 16.8 %collective-permute-start.2 = (bf16[256,2,2,128]{3,0,2,1:T(8,128)(2,1)S(1)}, bf16[256,2,2,128]{3,0,2,1:T(8,128)(2,1)}, u32[]{:S(2)}, u32[]{:S(2)}) collective-permute-start(bf16[256,2,2,128]{3,0,2,1:T(8,128)(2,1)S(1)} %copy.84), channel_id=1, source_target_pairs={{0,32},{16,48},{32,64},{48,80},{64,96},{80,112},{96,128},{112,144}... | collective-permute-start | bytes 786440 | tf_op jit(solution)/shard_map/ppermute | solution.py:14
  195.4 13.4 %collective-permute-start.3 = (bf16[256,2,2,128]{3,0,2,1:T(8,128)(2,1)S(1)}, bf16[256,2,2,128]{3,0,2,1:T(8,128)(2,1)S(1)}, u32[]{:S(2)}, u32[]{:S(2)}) collective-permute-start(bf16[256,2,2,128]{3,0,2,1:T(8,128)(2,1)S(1)} %copy.84), channel_id=1, source_target_pairs={{0,16},{16,32},{32,48},{48,64},{64,80},{80,96},{96,112},{112,128},... | collective-permute-start | bytes 786440 | tf_op jit(solution)/shard_map/ppermute | solution.py:14
  210.3 4.0 copy-start.4
  214.3 2.7 copy-start.2
  218.6 13.5 %collective-permute-start.7 = (bf16[256,2,2,128]{0,3,2,1:T(8,128)(2,1)S(1)}, bf16[256,2,2,128]{0,3,2,1:T(8,128)(2,1)S(1)}, u32[]{:S(2)}, u32[]{:S(2)}) collective-permute-start(bf16[256,2,2,128]{0,3,2,1:T(8,128)(2,1)S(1)} %get-tuple-element.258), channel_id=1, source_target_pairs={{64,0},{80,16},{96,32},{112,48},{128,64},{144,80},{160,96},{176,11... | collective-permute-start | bytes 786440 | tf_op jit(solution)/shard_map/ppermute | solution.py:14
  222.0 12.4 %collective-permute-start.6 = (bf16[256,2,2,128]{0,3,2,1:T(8,128)(2,1)S(1)}, bf16[256,2,2,128]{0,3,2,1:T(8,128)(2,1)S(1)}, u32[]{:S(2)}, u32[]{:S(2)}) collective-permute-start(bf16[256,2,2,128]{0,3,2,1:T(8,128)(2,1)S(1)} %get-tuple-element.259), channel_id=1, source_target_pairs={{48,0},{64,16},{80,32},{96,48},{112,64},{128,80},{144,96},{160,112... | collective-permute-start | bytes 786440 | tf_op jit(solution)/shard_map/ppermute | solution.py:14
  223.9 13.4 %collective-permute-start.5 = (bf16[256,2,2,128]{0,3,2,1:T(8,128)(2,1)S(1)}, bf16[256,2,2,128]{0,3,2,1:T(8,128)(2,1)S(1)}, u32[]{:S(2)}, u32[]{:S(2)}) collective-permute-start(bf16[256,2,2,128]{0,3,2,1:T(8,128)(2,1)S(1)} %get-tuple-element.260), channel_id=1, source_target_pairs={{32,0},{48,16},{64,32},{80,48},{96,64},{112,80},{128,96},{144,112}... | collective-permute-start | bytes 786440 | tf_op jit(solution)/shard_map/ppermute | solution.py:14
  225.9 14.3 %collective-permute-start.4 = (bf16[256,2,2,128]{0,3,2,1:T(8,128)(2,1)S(1)}, bf16[256,2,2,128]{0,3,2,1:T(8,128)(2,1)S(1)}, u32[]{:S(2)}, u32[]{:S(2)}) collective-permute-start(bf16[256,2,2,128]{0,3,2,1:T(8,128)(2,1)S(1)} %get-tuple-element.257), channel_id=1, source_target_pairs={{16,0},{32,16},{48,32},{64,48},{80,64},{96,80},{112,96},{128,112},... | collective-permute-start | bytes 786440 | tf_op jit(solution)/shard_map/ppermute | solution.py:14
  243.7 38.5 %all-to-all-start = ((bf16[256,16,256]{0,2,1:T(8,128)(2,1)}), bf16[256,16,256]{0,2,1:T(8,128)(2,1)}, u32[]{:S(2)}, u32[]{:S(2)}) async-start(bf16[256,16,256]{0,2,1:T(8,128)(2,1)} %bitcast.113), calls=%async_computation.1 | async-start | bytes 4194304 | tf_op jit(solution)/shard_map/all_to_all | solution.py:55
  251.0 158.1 %reduce-scatter.2.cloned.1.call-start = ((), (), s32[]{:S(2)}) async-start(), calls=%async_computation.2 | async-start | bytes 2228224 | tf_op jit(solution)/shard_map/reduce_scatter | solution.py:139
  286.1 3.4 copy-start.1
Sparse Core Ops, SparseCore 0:
  10.6 75.7 all-gather.7
  88.9 73.1 all-gather.9
  241.3 90.1 all-gather.5
  334.5 74.6 reduce-scatter.1
where the time goes:
time: 417 us; the launch traced here: 416 us
  waiting for transfers between devices  242 us (58%)
  local copies, waits for them, and re-layouts  54.6 us (13%)
  matrix products  53 us (13%)
  starting transfers between devices  31.7 us (8%)
  other arithmetic  16.4 us (4%)
  between operations  14 us (3%)
    all_gather x1, waiting for transfers between devices, on_device(): lax.all_gather(image_local, 'dp', axis=0, tiled=True)  74.8 us
    all_gather x1, waiting for transfers between devices, on_device(): lax.all_gather(text_local, 'dp', axis=0, tiled=True)  67.1 us
    all_to_all x1, waiting for transfers between devices, on_device(): lax.all_to_all(tokens, 'dp', split_axis=1, concat_axis=0, tiled=True)  30.8 us
    reduce_scatter x1, waiting for transfers between devices, on_device(): lax.psum_scatter(input_terms.astype(jnp.bfloat16), 'mp', scatter_dimensio...  27.9 us
    all_gather x1, waiting for transfers between devices, on_device(): gathered = lax.all_gather(dqkv, 'dp', axis=0, tiled=True)  26.7 us
    ppermute x8, starting transfers between devices, shifted(): return lax.ppermute(block, axis, route)  24.1 us
    dot_general x16, matrix products, accumulate(): jnp.einsum('bnf,bnc->bfc', column_group, grad_group, preferred_element_ty...  23.6 us
    while x3, local copies, waits for them, and re-layouts, blockwise(): result = lax.map(one_block, (blocks, modalities))  17.9 us
  transfers between devices with their start and end apart: 13, of which 9 were waited for; matrix products, arithmetic and copies ran while one was open for 22% of the time, Pallas kernels for 0%

commit v1 on v0

--- a/solution.py
+++ b/solution.py
@@ -1,3 +1,4 @@
+import functools
 import jax
 import jax.numpy as jnp
 from jax import lax
@@ -6,6 +7,21 @@
 HD = 128
 BLOCK = 128
 SPAN = 4
+
+
+def targets_pack(local_array, device_axis):
+    return jnp.concatenate(
+        lax.all_to_all(
+            jnp.stack([local_array] * lax.axis_size(device_axis), axis=0),
+            axis_name=device_axis,
+            split_axis=0,
+            concat_axis=0,
+        ),
+        axis=0,
+    )
+
+
+_follow_figure = functools.partial(targets_pack, device_axis="dp")
 
 
 def shifted(block, axis, distance):
@@ -55,7 +71,7 @@
     columns = lax.all_to_all(tokens, "dp", split_axis=1, concat_axis=0, tiled=True)
     text_whole, image_whole = (
         lax.all_gather(text_local, "dp", axis=0, tiled=True),
-        lax.all_gather(image_local, "dp", axis=0, tiled=True),
+        _follow_figure(image_local),
     )
     summed = blockwise(tokens, my_mods, text_whole, image_whole, 0)
     qkv = summed.astype(jnp.bfloat16).reshape(local_rows, 3, head_count, HD)

time: 417 us -> 389 us (0.933)
  waiting for transfers between devices: 242 us -> 212 us
  starting transfers between devices: 31.7 us -> 41.2 us
  local copies, waits for them, and re-layouts: 54.6 us -> 47.7 us
    all_gather x1 -> x0, waiting for transfers between devices: 74.8 us -> none  [on_device(): lax.all_gather(image_local, 'dp', axis=0, tiled=True)]
    all_gather x1, waiting for transfers between devices: 67.1 us -> 112 us  [on_device(): lax.all_gather(text_local, 'dp', axis=0, tiled=True)]
    while x3 -> x2, local copies, waits for them, and re-layouts: 17.9 us -> 9.2 us  [blockwise(): result = lax.map(one_block, (blocks, modalities))]
    all_to_all x0 -> x1, starting transfers between devices: none -> 7.58 us  [targets_pack(): lax.all_to_all(jnp.stack([local_array] * lax.axis_size(device_axis), axis...]
    unnamed x23 -> x21, local copies, waits for them, and re-layouts: 13.3 us -> 13.3 us
  transfers between devices with their start and end apart: 13 -> 13, of which waited for: 9 -> 9; matrix products, arithmetic and copies ran while one was open for 22% -> 24% of each run, Pallas kernels for 0% -> 0%
where the time goes in v1:
time: 389 us; the launch traced here: 388 us
  waiting for transfers between devices  212 us (54%)
  matrix products  53 us (14%)
  local copies, waits for them, and re-layouts  47.7 us (12%)
  starting transfers between devices  41.2 us (11%)
  other arithmetic  16.4 us (4%)
  between operations  14 us (4%)
    all_gather x1, waiting for transfers between devices, on_device(): lax.all_gather(text_local, 'dp', axis=0, tiled=True)  112 us
    all_to_all x1, waiting for transfers between devices, on_device(): lax.all_to_all(tokens, 'dp', split_axis=1, concat_axis=0, tiled=True)  30.8 us
    reduce_scatter x1, waiting for transfers between devices, on_device(): lax.psum_scatter(input_terms.astype(jnp.bfloat16), 'mp', scatter_dimensio...  28.1 us
    all_gather x1, waiting for transfers between devices, on_device(): gathered = lax.all_gather(dqkv, 'dp', axis=0, tiled=True)  26.5 us
    ppermute x8, starting transfers between devices, shifted(): return lax.ppermute(block, axis, route)  25.6 us
    dot_general x16, matrix products, accumulate(): jnp.einsum('bnf,bnc->bfc', column_group, grad_group, preferred_element_ty...  23.6 us
    dot_general x4, matrix products, select_product(): lax.dot_general(block_rows, text_mat, contraction, preferred_element_type...  17.6 us
    ppermute x8, waiting for transfers between devices, shifted(): return lax.ppermute(block, axis, route)  14.9 us
  transfers between devices with their start and end apart: 13, of which 9 were waited for; matrix products, arithmetic and copies ran while one was open for 24% of the time, Pallas kernels for 0%

profile of v1, /device:TPU:4, one launch (start us, length us, event | category | flops | bytes accessed | tf_op | source)
XLA Modules:
  0.0 387.8 jit_solution(2169783686246915007)
XLA Ops:
  13.7 7.6 %all-to-all-start = ((bf16[16,256,768]{2,1,0:T(8,128)(2,1)}), bf16[16,256,768]{2,1,0:T(8,128)(2,1)}, u32[]{:S(2)}, u32[]{:S(2)}) async-start(bf16[16,256,768]{2,1,0:T(8,128)(2,1)} %stack.12), calls=%async_computation | async-start | bytes 12582912 | tf_op jit(solution)/shard_map/all_to_all | solution.py:14
  21.6 111.6 %all-gather.6.cloned.1.call-done = bf16[4096,1,768]{0,2,1:T(8,128)(2,1)} async-done(((bf16[256,1,768]{0,2,1:T(8,128)(2,1)}), bf16[4096,1,768]{0,2,1:T(8,128)(2,1)}) %all-gather.6.cloned.1.call-update) | async-done | bytes 6291472 | tf_op jit(solution)/shard_map/all_gather | solution.py:73
  133.2 8.8 %copy.58 = bf16[4096,768]{1,0:T(8,128)(2,1)} copy(bf16[4096,768]{0,1:T(8,128)(2,1)} %bitcast.116) | data formatting | bytes 12582912 | tf_op jit(solution)/shard_map/while | solution.py:52
  142.0 10.4 %while.31 = (s32[]{:T(128)}, bf16[2,128,768]{2,1,0:T(8,128)(2,1)S(1)}, s32[2]{0:T(128)S(1)}, bf16[2,128,4096]{2,1,0:T(8,128)(2,1)S(1)}, bf16[4096,768]{1,0:T(8,1...) while((s32[]{:T(128)}, bf16[2,128,768]{2,1,0:T(8,128)(2,1)S(1)}, s32[2]{0:T(128)S(1)}, ...), condition=%wide.region_3.4_spmd, body=%wide.region_0.3_spmd.sunk | while | flops 805306368 | bytes 10027175 | solution.py:52
  143.3 3.8 conditional.4
  143.3 3.8 convolution_bitcast_fusion.1
  148.5 3.8 conditional.4
  148.6 3.8 convolution_bitcast_fusion.1
  155.4 6.6 %collective-permute-start.1 = (bf16[256,2,2,128]{3,0,2,1:T(8,128)(2,1)S(1)}, bf16[256,2,2,128]{3,0,2,1:T(8,128)(2,1)}, u32[]{:S(2)}, u32[]{:S(2)}) collective-permute-start(bf16[256,2,2,128]{3,0,2,1:T(8,128)(2,1)S(1)} %copy.81), channel_id=1, source_target_pairs={{0,48},{16,64},{32,80},{48,96},{64,112},{80,128},{96,144},{112,160... | collective-permute-start | bytes 786440 | tf_op jit(solution)/shard_map/ppermute | solution.py:30
  171.8 6.2 %collective-permute-done.2 = bf16[256,2,2,128]{3,0,2,1:T(8,128)(2,1)} collective-permute-done((bf16[256,2,2,128]{3,0,2,1:T(8,128)(2,1)S(1)}, bf16[256,2,2,128]{3,0,2,1:T(8,128)(2,1)}, u32[]{:S(2)}, u32[]{:S(2)}) %collective-permute-start.2) | collective-permute-done | bytes 262176 | tf_op jit(solution)/shard_map/ppermute | solution.py:30
  181.8 4.0 %fusion.30 = (f32[2,256]{1,0:T(2,128)S(1)}, f32[2,256,1280]{2,1,0:T(8,128)}) fusion(pred[256,1280]{1,0:T(8,128)(4,1)S(1)} %fusion.16, bf16[1280,2,2,128]{3,0,2,1:T(8,128)(2,1)} %constant_dynamic-update-slice_fusion.2, bf16[256,1,2,128]{3,2,1,0:T(2,128)(2,1)S(1)} %slice.52), kind=kOutput, calls=%fused_computation.66 | convolution fusion | flops 171050240 | bytes 4065280 | tf_op jit(solution)/shard_map/sub | solution.py:99
  197.6 4.6 %collective-permute-start.4 = (bf16[256,2,2,128]{0,3,2,1:T(8,128)(2,1)S(1)}, bf16[256,2,2,128]{0,3,2,1:T(8,128)(2,1)S(1)}, u32[]{:S(2)}, u32[]{:S(2)}) collective-permute-start(bf16[256,2,2,128]{0,3,2,1:T(8,128)(2,1)S(1)} %get-tuple-element.257), channel_id=1, source_target_pairs={{16,0},{32,16},{48,32},{64,48},{80,64},{96,80},{112,96},{128,112},... | collective-permute-start | bytes 786440 | tf_op jit(solution)/shard_map/ppermute | solution.py:30
  215.5 7.7 %all-to-all-start.1 = ((bf16[256,16,256]{0,2,1:T(8,128)(2,1)}), bf16[256,16,256]{0,2,1:T(8,128)(2,1)}, u32[]{:S(2)}, u32[]{:S(2)}) async-start(bf16[256,16,256]{0,2,1:T(8,128)(2,1)} %bitcast.115), calls=%async_computation.2 | async-start | bytes 4194304 | tf_op jit(solution)/shard_map/all_to_all | solution.py:71
  223.5 30.8 %all-to-all-done.1 = bf16[256,16,256]{0,2,1:T(8,128)(2,1)} async-done(((bf16[256,16,256]{0,2,1:T(8,128)(2,1)}), bf16[256,16,256]{0,2,1:T(8,128)(2,1)}, u32[]{:S(2)}, u32[]{:S(2)}) %all-to-all-start.1) | async-done | bytes 2097184 | tf_op jit(solution)/shard_map/all_to_all | solution.py:71
  254.3 3.9 %copy.70 = bf16[16,256,256]{2,1,0:T(8,128)(2,1)} copy(bf16[16,256,256]{1,2,0:T(8,128)(2,1)} %bitcast.27) | data formatting | bytes 4194304 | tf_op jit(solution)/shard_map/all_to_all | solution.py:71
  262.2 14.8 %while.32 = (s32[]{:T(128)}, bf16[2,128,4096]{2,1,0:T(8,128)(2,1)}, s32[2]{0:T(128)S(1)}, bf16[2,128,768]{2,1,0:T(8,128)(2,1)S(1)}, bf16[4096,768]{1,0:T(8,128)(...) while((s32[]{:T(128)}, bf16[2,128,4096]{2,1,0:T(8,128)(2,1)}, s32[2]{0:T(128)S(1)}, ...), condition=%wide.region_10.11_spmd, body=%wide.region_7.10_spmd.sunk | while | flops 805306368 | bytes 10027175 | solution.py:52
  263.5 4.9 %conditional.5 = (bf16[1,128,4096]{2,1,0:T(8,128)(2,1)S(1)}) conditional(s32[]{:T(128)} %bitcast.108, (bf16[128,768]{1,0:T(8,128)(2,1)S(1)}, bf16[4096,768]{1,0:T(8,128)(2,1)}) %tuple.94, (bf16[128,768]{1,0:T(8,128)(2,1)S(1)}, bf16[4096,768]{1,0:T(8,128)(2,1)}) %tuple.95), branch_computations={%region_8.8_spmd, %region_9.9_spmd} | conditional | flops 805306368 | bytes 7536648 | solution.py:35
  263.5 4.9 %convolution_bitcast_fusion.3 = bf16[1,128,4096]{2,1,0:T(8,128)(2,1)S(1)} fusion(bf16[128,768]{1,0:T(8,128)(2,1)S(1)} %get-tuple-element.109, bf16[4096,768]{1,0:T(8,128)(2,1)} %get-tuple-element.110), kind=kOutput, calls=%fused_computation.6 | convolution fusion | flops 805306368 | bytes 7536640 | tf_op jit(solution)/shard_map/while/body/eval_jaxpr/cond/branch_1_fun/dot_general | solution.py:37
  270.8 5.1 %conditional.5 = (bf16[1,128,4096]{2,1,0:T(8,128)(2,1)S(1)}) conditional(s32[]{:T(128)} %bitcast.108, (bf16[128,768]{1,0:T(8,128)(2,1)S(1)}, bf16[4096,768]{1,0:T(8,128)(2,1)}) %tuple.94, (bf16[128,768]{1,0:T(8,128)(2,1)S(1)}, bf16[4096,768]{1,0:T(8,128)(2,1)}) %tuple.95), branch_computations={%region_8.8_spmd, %region_9.9_spmd} | conditional | flops 805306368 | bytes 7536648 | solution.py:35
  270.8 5.0 %convolution_bitcast_fusion.3 = bf16[1,128,4096]{2,1,0:T(8,128)(2,1)S(1)} fusion(bf16[128,768]{1,0:T(8,128)(2,1)S(1)} %get-tuple-element.109, bf16[4096,768]{1,0:T(8,128)(2,1)} %get-tuple-element.110), kind=kOutput, calls=%fused_computation.6 | convolution fusion | flops 805306368 | bytes 7536640 | tf_op jit(solution)/shard_map/while/body/eval_jaxpr/cond/branch_1_fun/dot_general | solution.py:37
  277.0 26.5 %all-gather.4.cloned.1.call-done = bf16[4096,768]{0,1:T(8,128)(2,1)} async-done(((bf16[256,768]{0,1:T(8,128)(2,1)}), bf16[4096,768]{0,1:T(8,128)(2,1)}) %all-gather.4.cloned.1.call-update) | async-done | bytes 6291472 | tf_op jit(solution)/shard_map/all_gather | solution.py:130
  303.5 8.6 %copy.71 = bf16[4096,768]{1,0:T(8,128)(2,1)} copy(bf16[4096,768]{0,1:T(8,128)(2,1)} %all-gather.4.cloned.1.call-done) | data formatting | bytes 12582912 | tf_op jit(solution)/shard_map/all_gather | solution.py:130
  312.1 39.0 %while.33 = (s32[]{:T(128)}, f32[2,256,768]{2,1,0:T(8,128)S(1)}, s32[16,2]{1,0:T(8,128)S(1)}, bf16[16,2,128,256]{3,2,1,0:T(8,128)(2,1)}, bf16[16,2,128,768]{3,2,1,0:T(8,128)(2,1)}, /*index=5*/s32[]{:T(128)}, s32[]{:T(128)}) while((s32[]{:T(128)}, f32[2,256,768]{2,1,0:T(8,128)S(1)}, s32[16,2]{1,0:T(8,128)S(1)}, ...), condition=%wide.region_14.15_spmd.clone, body=%wide.region_12.14_spmd.clone.sunk | while | flops 102629384 | bytes 9962651 | solution.py:144
  353.2 28.1 %reduce-scatter.2.cloned.1.call-done = bf16[256,256]{1,0:T(8,128)(2,1)} async-done(((bf16[256,4096]{1,0:T(8,128)(2,1)}), bf16[256,256]{1,0:T(8,128)(2,1)}) %reduce-scatter.2.cloned.1.call-update) | async-done | bytes 131088 | tf_op jit(solution)/shard_map/reduce_scatter | solution.py:155
  (162 shorter events, 97.7 us)
Async XLA Ops:
  7.2 126.1 %all-gather.6.cloned.1.call-start = ((), (), s32[]{:S(2)}) async-start(), calls=%async_computation.5 | async-start | bytes 6684672 | tf_op jit(solution)/shard_map/all_gather | solution.py:73
  13.7 7.7 %copy-start.5 = (s32[32]{0:T(128)S(1)}, s32[32]{0:T(128)}, u32[]{:S(2)}) copy-start(s32[32]{0:T(128)} %param.17) | copy-start | bytes 388
  13.7 7.7 %copy-start.4 = (s32[4096]{0:T(1024)S(1)}, s32[4096]{0:T(1024)}, u32[]{:S(2)}) copy-start(s32[4096]{0:T(1024)} %param.18) | copy-start | bytes 49156
  13.7 128.3 %all-to-all-start = ((bf16[16,256,768]{2,1,0:T(8,128)(2,1)}), bf16[16,256,768]{2,1,0:T(8,128)(2,1)}, u32[]{:S(2)}, u32[]{:S(2)}) async-start(bf16[16,256,768]{2,1,0:T(8,128)(2,1)} %stack.12), calls=%async_computation | async-start | bytes 12582912 | tf_op jit(solution)/shard_map/all_to_all | solution.py:14
  21.3 282.2 %all-gather.4.cloned.1.call-start = ((), (), s32[]{:S(2)}) async-start(), calls=%async_computation.4 | async-start | bytes 6684672 | tf_op jit(solution)/shard_map/all_gather | solution.py:130
  133.2 8.8 %copy-start = (bf16[256,4096]{1,0:T(8,128)(2,1)S(1)}, bf16[256,4096]{1,0:T(8,128)(2,1)}, u32[]{:S(2)}) copy-start(bf16[256,4096]{1,0:T(8,128)(2,1)} %param.15) | copy-start | bytes 6291460
  152.8 15.6 %collective-permute-start = (bf16[256,2,2,128]{3,0,2,1:T(8,128)(2,1)S(1)}, bf16[256,2,2,128]{3,0,2,1:T(8,128)(2,1)}, u32[]{:S(2)}, u32[]{:S(2)}) collective-permute-start(bf16[256,2,2,128]{3,0,2,1:T(8,128)(2,1)S(1)} %copy.81), channel_id=1, source_target_pairs={{0,64},{16,80},{32,96},{48,112},{64,128},{80,144},{96,160},{112,17... | collective-permute-start | bytes 786440 | tf_op jit(solution)/shard_map/ppermute | solution.py:30
  155.4 14.7 %collective-permute-start.1 = (bf16[256,2,2,128]{3,0,2,1:T(8,128)(2,1)S(1)}, bf16[256,2,2,128]{3,0,2,1:T(8,128)(2,1)}, u32[]{:S(2)}, u32[]{:S(2)}) collective-permute-start(bf16[256,2,2,128]{3,0,2,1:T(8,128)(2,1)S(1)} %copy.81), channel_id=1, source_target_pairs={{0,48},{16,64},{32,80},{48,96},{64,112},{80,128},{96,144},{112,160... | collective-permute-start | bytes 786440 | tf_op jit(solution)/shard_map/ppermute | solution.py:30
  162.0 15.9 %collective-permute-start.2 = (bf16[256,2,2,128]{3,0,2,1:T(8,128)(2,1)S(1)}, bf16[256,2,2,128]{3,0,2,1:T(8,128)(2,1)}, u32[]{:S(2)}, u32[]{:S(2)}) collective-permute-start(bf16[256,2,2,128]{3,0,2,1:T(8,128)(2,1)S(1)} %copy.81), channel_id=1, source_target_pairs={{0,32},{16,48},{32,64},{48,80},{64,96},{80,112},{96,128},{112,144}... | collective-permute-start | bytes 786440 | tf_op jit(solution)/shard_map/ppermute | solution.py:30
  166.3 14.0 %collective-permute-start.3 = (bf16[256,2,2,128]{3,0,2,1:T(8,128)(2,1)S(1)}, bf16[256,2,2,128]{3,0,2,1:T(8,128)(2,1)S(1)}, u32[]{:S(2)}, u32[]{:S(2)}) collective-permute-start(bf16[256,2,2,128]{3,0,2,1:T(8,128)(2,1)S(1)} %copy.81), channel_id=1, source_target_pairs={{0,16},{16,32},{32,48},{48,64},{64,80},{80,96},{96,112},{112,128},... | collective-permute-start | bytes 786440 | tf_op jit(solution)/shard_map/ppermute | solution.py:30
  181.8 4.0 %copy-start.3 = (bf16[256,256]{0,1:T(8,128)(2,1)S(1)}, bf16[256,256]{0,1:T(8,128)(2,1)}, u32[]{:S(2)}) copy-start(bf16[256,256]{0,1:T(8,128)(2,1)} %copy.83) | copy-start | bytes 393220
  185.8 2.7 copy-start.2
  190.1 13.8 %collective-permute-start.7 = (bf16[256,2,2,128]{0,3,2,1:T(8,128)(2,1)S(1)}, bf16[256,2,2,128]{0,3,2,1:T(8,128)(2,1)S(1)}, u32[]{:S(2)}, u32[]{:S(2)}) collective-permute-start(bf16[256,2,2,128]{0,3,2,1:T(8,128)(2,1)S(1)} %get-tuple-element.258), channel_id=1, source_target_pairs={{64,0},{80,16},{96,32},{112,48},{128,64},{144,80},{160,96},{176,11... | collective-permute-start | bytes 786440 | tf_op jit(solution)/shard_map/ppermute | solution.py:30
  193.8 12.4 %collective-permute-start.6 = (bf16[256,2,2,128]{0,3,2,1:T(8,128)(2,1)S(1)}, bf16[256,2,2,128]{0,3,2,1:T(8,128)(2,1)S(1)}, u32[]{:S(2)}, u32[]{:S(2)}) collective-permute-start(bf16[256,2,2,128]{0,3,2,1:T(8,128)(2,1)S(1)} %get-tuple-element.259), channel_id=1, source_target_pairs={{48,0},{64,16},{80,32},{96,48},{112,64},{128,80},{144,96},{160,112... | collective-permute-start | bytes 786440 | tf_op jit(solution)/shard_map/ppermute | solution.py:30
  195.7 13.5 %collective-permute-start.5 = (bf16[256,2,2,128]{0,3,2,1:T(8,128)(2,1)S(1)}, bf16[256,2,2,128]{0,3,2,1:T(8,128)(2,1)S(1)}, u32[]{:S(2)}, u32[]{:S(2)}) collective-permute-start(bf16[256,2,2,128]{0,3,2,1:T(8,128)(2,1)S(1)} %get-tuple-element.260), channel_id=1, source_target_pairs={{32,0},{48,16},{64,32},{80,48},{96,64},{112,80},{128,96},{144,112}... | collective-permute-start | bytes 786440 | tf_op jit(solution)/shard_map/ppermute | solution.py:30
  197.6 14.4 %collective-permute-start.4 = (bf16[256,2,2,128]{0,3,2,1:T(8,128)(2,1)S(1)}, bf16[256,2,2,128]{0,3,2,1:T(8,128)(2,1)S(1)}, u32[]{:S(2)}, u32[]{:S(2)}) collective-permute-start(bf16[256,2,2,128]{0,3,2,1:T(8,128)(2,1)S(1)} %get-tuple-element.257), channel_id=1, source_target_pairs={{16,0},{32,16},{48,32},{64,48},{80,64},{96,80},{112,96},{128,112},... | collective-permute-start | bytes 786440 | tf_op jit(solution)/shard_map/ppermute | solution.py:30
  215.5 38.8 %all-to-all-start.1 = ((bf16[256,16,256]{0,2,1:T(8,128)(2,1)}), bf16[256,16,256]{0,2,1:T(8,128)(2,1)}, u32[]{:S(2)}, u32[]{:S(2)}) async-start(bf16[256,16,256]{0,2,1:T(8,128)(2,1)} %bitcast.115), calls=%async_computation.2 | async-start | bytes 4194304 | tf_op jit(solution)/shard_map/all_to_all | solution.py:71
  223.2 158.1 %reduce-scatter.2.cloned.1.call-start = ((), (), s32[]{:S(2)}) async-start(), calls=%async_computation.3 | async-start | bytes 2228224 | tf_op jit(solution)/shard_map/reduce_scatter | solution.py:155
  258.2 3.4 copy-start.1
Sparse Core Ops, SparseCore 0:
  11.1 122.0 all-gather.5
  213.1 90.3 all-gather.3
  306.6 74.6 reduce-scatter.1
